TPU v7x, 32 devices: a whole 2x2x4 slice. The times are simulated.
32 devices in a mesh: species: 4 (over z), space: 8 (over y, x, core).
Axes of the slice: x: 2, y: 2, z: 4, core: 2. Of those that a mesh axis runs over, the one named last changes fastest.
Arguments:
- density: float32 [4, 32, 16, 32, 128], P('species', None, 'space'), may hold values from 0 to 2
- space_factor: float32 [16, 32, 128], P('space'), may hold values from 0.5 to 1
- diff_rate: float32 [4, 32], P('species'), may hold values from 0.02 to 0.08
- loss_inverse: float32 [4, 32, 32], P('species'), may hold values from 0 to 1, as said below
- chain_yield: float32 [4, 32], P('species'), may hold values from 0.25 to 0.95
- survival: float32 [4, 32], P('species'), may hold values from 0.6 to 1
- gamma_yield: float32 [4, 32], P('species'), may hold values from 0.1 to 1
- sky_weight: bfloat16 [8, 8, 64, 128], P('space'), may hold values from -0.75 to 0.75
- sky_blocks: int32 [8, 8], P('space'), may hold values from 0 to 383
Outputs:
- propagated: float32 [4, 32, 16, 32, 128], P('species', None, 'space')
- sky: float32 [384, 128], P('space')
Inputs may be any that keep to these rules, and one draw needn't show every extreme that they name: `loss_inverse`: each matrix is upper triangular with a diagonal of 0.5 to 1 and nonnegative entries.
All inputs are finite; a program needn't handle non-finite values.
Results may differ from a plain program's by a relative error of at most 0.0011.
Values sent between devices are 32-bit elements; how exact they have to be, the bound alone decides.
No kernel may reach another device: no remote copies, remote signals or barrier semaphores. Data moves between devices by JAX's collectives and lax.ppermute only.
A program may use at most 64 MiB of HBM per device.

v0:
```python
import jax
import jax.numpy as jnp
from jax import lax
from jax.sharding import PartitionSpec as P

SUBSTEPS = 2
NB = 384


def padded_2(cells, sides, width):
    for axis, dim in sides:
        count = lax.axis_size(axis)
        ends = count - 1
        head = lax.slice_in_dim(cells, 0, width, axis=dim)
        tail = lax.slice_in_dim(cells, cells.shape[dim] - width, cells.shape[dim], axis=dim)
        cells = jnp.concatenate(
            [
                lax.ppermute(tail, axis, [(i, (i + 1) % count) for i in range(ends)]),
                cells,
                lax.ppermute(head, axis, [((i + 1) % count, i) for i in range(ends)]),
            ],
            axis=dim,
        )
    return cells


def from_behind(block, axis, distance):
    devices = range(lax.axis_size(axis))
    route = [(i - distance, i) for i in devices if i - distance in devices]
    return lax.ppermute(block, axis, route)


def cross_sum(field):
    padded = jnp.pad(field, ((0, 0), (0, 0), (1, 1), (1, 1)))
    beside = padded[:, :, 2:, 1:-1] + padded[:, :, :-2, 1:-1]
    beside = beside + padded[:, :, 1:-1, 2:] + padded[:, :, 1:-1, :-2]
    return beside


def body(
    density,
    space_factor,
    diff_rate,
    loss_inverse,
    chain_yield,
    survival,
    gamma_yield,
    sky_weight,
    sky_blocks,
):
    field = density[0]
    bins = field.shape[0]
    width = field.shape[1]
    rate = diff_rate[0][:, None, None, None]
    factor = rate * space_factor[None]
    for step in range(SUBSTEPS):
        wider = padded_2(field, (("space", 1),), 1)
        beside = wider[:, 2:] + wider[:, :-2] + cross_sum(field)
        field = field + factor * (beside - 6.0 * field)
    solved = jnp.dot(
        loss_inverse[0],
        field.reshape(bins, -1),
        precision=lax.Precision.HIGHEST,
        preferred_element_type=jnp.float32,
    ).reshape(field.shape)
    factor_chain = chain_yield[0][:, None, None, None]
    own_part = survival[0][:, None, None, None] * solved
    carried = own_part
    for section in range(lax.axis_size("species") - 1):
        carried = factor_chain * from_behind(carried, "species", 1) + own_part
    weighted = jnp.dot(
        gamma_yield[0],
        carried.reshape(bins, -1),
        precision=lax.Precision.HIGHEST,
        preferred_element_type=jnp.float32,
    )
    depth = carried.shape[3]
    emission = (
        jnp.sum(weighted.reshape(width, carried.shape[2], depth), axis=2) / (bins * depth)
    ).astype(jnp.bfloat16)
    columns = emission.reshape(-1)
    contribution = jnp.einsum(
        "c,lcb->lb", columns, sky_weight[0], preferred_element_type=jnp.float32
    )
    onehot = (sky_blocks[0][:, None] == jnp.arange(NB, dtype=jnp.int32)[None, :]).astype(
        jnp.float32
    )
    dense_map = jnp.dot(
        onehot.T, contribution, precision=lax.Precision.HIGHEST, preferred_element_type=jnp.float32
    )
    summed = lax.psum(dense_map, "species")
    sky = lax.psum_scatter(summed, "space", scatter_dimension=0, tiled=True)
    return (carried[None], sky)


def solution(mesh):
    placed = (
        P("species", None, "space", None, None),
        P("space", None, None),
        P("species", None),
        P("species", None, None),
        P("species", None),
        P("species", None),
        P("species", None),
        P("space", None, None, None),
        P("space", None),
    )
    return jax.shard_map(
        body,
        mesh=mesh,
        in_specs=placed,
        out_specs=(P("species", None, "space", None, None), P("space", None)),
        check_vma=False,
    )
```

profile of v0, /device:TPU:0, one launch (start us, length us, event | category | flops | bytes accessed | tf_op | source)
XLA Modules:
  0.0 190.8 jit_solution(6497044509966995586)
XLA Ops:
  7.2 0.0 copy-start
  7.2 0.0 reduce-scatter.2.cloned.1.call-start
  7.2 0.0 copy-start.1
  7.2 0.0 copy-start.3
  7.2 0.0 copy-start.7
  7.3 1.4 fusion.25
  8.6 1.3 collective-permute-start
  9.9 3.1 %collective-permute-start.1 = (f32[32,1,32,128]{3,2,1,0:T(8,128)S(1)}, f32[32,1,32,128]{3,2,1,0:T(8,128)S(1)}, u32[]{:S(2)}, u32[]{:S(2)}) collective-permute-start(f32[32,1,32,128]{3,2,1,0:T(8,128)S(1)} %get-tuple-element.5), channel_id=1, source_target_pairs={{0,1},{1,2},{2,3},{3,4},{4,5},{5,6},{6,7},{8,9},{9,10},{10,11},{11... | collective-permute-start | bytes 1572872 | tf_op jit(solution)/shard_map/ppermute | solution.py:18
  13.0 0.0 collective-permute-done
  13.0 1.5 collective-permute-done.1
  14.5 0.0 copy-done.1
  14.5 0.0 copy-done.3
  14.5 0.0 copy-done.7
  14.5 0.8 fusion
  15.3 0.1 fusion.24
  15.4 1.3 collective-permute-start.2
  16.7 0.0 copy-start.4
  16.7 10.4 %collective-permute-start.3 = (f32[32,1,32,128]{3,2,1,0:T(8,128)S(1)}, f32[32,1,32,128]{3,2,1,0:T(8,128)S(1)}, u32[]{:S(2)}, u32[]{:S(2)}) collective-permute-start(f32[32,1,32,128]{3,2,1,0:T(8,128)S(1)} %get-tuple-element.3), channel_id=1, source_target_pairs={{0,1},{1,2},{2,3},{3,4},{4,5},{5,6},{6,7},{8,9},{9,10},{10,11},{11... | collective-permute-start | bytes 1572872 | tf_op jit(solution)/shard_map/ppermute | solution.py:18
  27.1 0.0 collective-permute-done.2
  27.1 1.5 collective-permute-done.3
  28.6 0.8 fusion.1
  29.4 0.0 copy-done.4
  29.4 1.7 convolution_bitcast_fusion
  31.1 0.0 copy-start.5
  31.1 0.2 copy.16
  31.3 0.5 copy-done.5
  31.7 0.0 copy-start.6
  31.7 0.1 broadcast_multiply_fusion
  31.9 3.5 %collective-permute-start.4 = (f32[32,2,32,128]{3,2,1,0:T(8,128)S(1)}, f32[32,2,32,128]{3,2,1,0:T(8,128)S(1)}, u32[]{:S(2)}, u32[]{:S(2)}) collective-permute-start(f32[32,2,32,128]{3,2,1,0:T(8,128)S(1)} %broadcast_multiply_fusion), channel_id=1, source_target_pairs={{0,8},{8,16},{16,24},{1,9},{9,17},{17,25},{2,10},{10,18},{18,26},{... | collective-permute-start | bytes 3145736 | tf_op jit(solution)/shard_map/ppermute | solution.py:30
  35.4 18.0 %collective-permute-done.4 = f32[32,2,32,128]{3,2,1,0:T(8,128)S(1)} collective-permute-done((f32[32,2,32,128]{3,2,1,0:T(8,128)S(1)}, f32[32,2,32,128]{3,2,1,0:T(8,128)S(1)}, u32[]{:S(2)}, u32[]{:S(2)}) %collective-permute-start.4) | collective-permute-done | bytes 1048608 | tf_op jit(solution)/shard_map/ppermute | solution.py:30
  53.4 0.0 copy-done.6
  53.4 0.2 multiply_add_fusion.2
  53.6 4.5 %collective-permute-start.5 = (f32[32,2,32,128]{3,2,1,0:T(8,128)S(1)}, f32[32,2,32,128]{3,2,1,0:T(8,128)S(1)}, u32[]{:S(2)}, u32[]{:S(2)}) collective-permute-start(f32[32,2,32,128]{3,2,1,0:T(8,128)S(1)} %multiply_add_fusion.2), channel_id=1, source_target_pairs={{0,8},{8,16},{16,24},{1,9},{9,17},{17,25},{2,10},{10,18},{18,26},{... | collective-permute-start | bytes 3145736 | tf_op jit(solution)/shard_map/ppermute | solution.py:30
  58.1 19.1 %collective-permute-done.5 = f32[32,2,32,128]{3,2,1,0:T(8,128)S(1)} collective-permute-done((f32[32,2,32,128]{3,2,1,0:T(8,128)S(1)}, f32[32,2,32,128]{3,2,1,0:T(8,128)S(1)}, u32[]{:S(2)}, u32[]{:S(2)}) %collective-permute-start.5) | collective-permute-done | bytes 1048608 | tf_op jit(solution)/shard_map/ppermute | solution.py:30
  77.1 0.2 multiply_add_fusion.1
  77.3 4.5 %collective-permute-start.6 = (f32[32,2,32,128]{3,2,1,0:T(8,128)S(1)}, f32[32,2,32,128]{3,2,1,0:T(8,128)S(1)}, u32[]{:S(2)}, u32[]{:S(2)}) collective-permute-start(f32[32,2,32,128]{3,2,1,0:T(8,128)S(1)} %multiply_add_fusion.1), channel_id=1, source_target_pairs={{0,8},{8,16},{16,24},{1,9},{9,17},{17,25},{2,10},{10,18},{18,26},{... | collective-permute-start | bytes 3145736 | tf_op jit(solution)/shard_map/ppermute | solution.py:30
  81.8 20.1 %collective-permute-done.6 = f32[32,2,32,128]{3,2,1,0:T(8,128)S(1)} collective-permute-done((f32[32,2,32,128]{3,2,1,0:T(8,128)S(1)}, f32[32,2,32,128]{3,2,1,0:T(8,128)S(1)}, u32[]{:S(2)}, u32[]{:S(2)}) %collective-permute-start.6) | collective-permute-done | bytes 1048608 | tf_op jit(solution)/shard_map/ppermute | solution.py:30
  101.9 0.2 multiply_add_fusion
  102.1 0.0 copy-start.2
  102.1 0.6 copy.26
  102.7 0.3 copy-done.2
  103.1 0.0 copy-start.8
  103.1 0.2 copy.18
  103.3 0.0 copy-start.9
  103.3 0.5 copy-done.8
  103.7 1.2 fusion.16
  105.0 0.1 reduce_sum.9
  105.1 0.1 reshape.34
  105.2 0.0 copy-done
  105.2 0.1 fusion.18
  105.3 0.0 copy-done.9
  105.3 1.1 fusion.21
  106.4 0.0 reduce-scatter.2.cloned.1.call-update
  106.4 57.4 %reduce-scatter.2.cloned.1.call-done = f32[48,128]{1,0:T(8,128)} async-done(((f32[384,128]{1,0:T(8,128)}), f32[48,128]{1,0:T(8,128)}) %reduce-scatter.2.cloned.1.call-update) | async-done | bytes 24592 | tf_op jit(solution)/shard_map/reduce_scatter | solution.py:92
  163.8 20.2 %psum.8 = f32[48,128]{1,0:T(8,128)} all-reduce(f32[48,128]{1,0:T(8,128)} %reduce-scatter.2.cloned.1.call-done), channel_id=1, replica_groups=mesh['species'=4,'space'=8] {'species'}, use_global_device_ids=true, to_apply=%region_1.2 | all-reduce | flops 6144 | bytes 49152 | tf_op jit(solution)/shard_map/psum | solution.py:91
  (1 shorter events, 0.0 us)
Async XLA Ops:
  7.2 98.0 %copy-start = (bf16[1,8,64,128]{3,2,1,0:T(8,128)(2,1)S(1)}, bf16[1,8,64,128]{3,2,1,0:T(8,128)(2,1)}, u32[]{:S(2)}) copy-start(bf16[1,8,64,128]{3,2,1,0:T(8,128)(2,1)} %param.16) | copy-start | bytes 393220
  7.2 156.6 %reduce-scatter.2.cloned.1.call-start = ((), (), s32[]{:S(2)}) async-start(), calls=%async_computation.1 | async-start | bytes 221184 | tf_op jit(solution)/shard_map/reduce_scatter | solution.py:92
  7.2 7.3 %copy-start.1 = (f32[1,32,2,32,128]{4,3,2,1,0:T(8,128)S(1)}, f32[1,32,2,32,128]{4,3,2,1,0:T(8,128)}, u32[]{:S(2)}) copy-start(f32[1,32,2,32,128]{4,3,2,1,0:T(8,128)} %param.9) | copy-start | bytes 3145732
  7.2 7.3 %copy-start.3 = (f32[2,32,128]{2,1,0:T(8,128)S(1)}, f32[2,32,128]{2,1,0:T(8,128)}, u32[]{:S(2)}) copy-start(f32[2,32,128]{2,1,0:T(8,128)} %param.10) | copy-start | bytes 98308
  7.2 7.2 %copy-start.7 = (f32[1,32]{1,0:T(1,128)S(1)}, f32[1,32]{1,0:T(1,128)}, u32[]{:S(2)}) copy-start(f32[1,32]{1,0:T(1,128)} %param.11) | copy-start | bytes 388
  8.6 4.4 %collective-permute-start = (f32[32,1,32,128]{3,2,1,0:T(8,128)S(1)}, f32[32,1,32,128]{3,2,1,0:T(8,128)S(1)}, u32[]{:S(2)}, u32[]{:S(2)}) collective-permute-start(f32[32,1,32,128]{3,2,1,0:T(8,128)S(1)} %get-tuple-element.4), channel_id=1, source_target_pairs={{1,0},{2,1},{3,2},{4,3},{5,4},{6,5},{7,6},{9,8},{10,9},{11,10},{12... | collective-permute-start | bytes 1572872 | tf_op jit(solution)/shard_map/ppermute | solution.py:20
  9.9 4.6 %collective-permute-start.1 = (f32[32,1,32,128]{3,2,1,0:T(8,128)S(1)}, f32[32,1,32,128]{3,2,1,0:T(8,128)S(1)}, u32[]{:S(2)}, u32[]{:S(2)}) collective-permute-start(f32[32,1,32,128]{3,2,1,0:T(8,128)S(1)} %get-tuple-element.5), channel_id=1, source_target_pairs={{0,1},{1,2},{2,3},{3,4},{4,5},{5,6},{6,7},{8,9},{9,10},{10,11},{11... | collective-permute-start | bytes 1572872 | tf_op jit(solution)/shard_map/ppermute | solution.py:18
  15.4 11.7 %collective-permute-start.2 = (f32[32,1,32,128]{3,2,1,0:T(8,128)S(1)}, f32[32,1,32,128]{3,2,1,0:T(8,128)S(1)}, u32[]{:S(2)}, u32[]{:S(2)}) collective-permute-start(f32[32,1,32,128]{3,2,1,0:T(8,128)S(1)} %get-tuple-element.2), channel_id=1, source_target_pairs={{1,0},{2,1},{3,2},{4,3},{5,4},{6,5},{7,6},{9,8},{10,9},{11,10},{12... | collective-permute-start | bytes 1572872 | tf_op jit(solution)/shard_map/ppermute | solution.py:20
  16.7 12.7 %copy-start.4 = (f32[1,32,32]{2,1,0:T(8,128)S(1)}, f32[1,32,32]{2,1,0:T(8,128)}, u32[]{:S(2)}) copy-start(f32[1,32,32]{2,1,0:T(8,128)} %param.12) | copy-start | bytes 12292
  16.7 11.9 %collective-permute-start.3 = (f32[32,1,32,128]{3,2,1,0:T(8,128)S(1)}, f32[32,1,32,128]{3,2,1,0:T(8,128)S(1)}, u32[]{:S(2)}, u32[]{:S(2)}) collective-permute-start(f32[32,1,32,128]{3,2,1,0:T(8,128)S(1)} %get-tuple-element.3), channel_id=1, source_target_pairs={{0,1},{1,2},{2,3},{3,4},{4,5},{5,6},{6,7},{8,9},{9,10},{10,11},{11... | collective-permute-start | bytes 1572872 | tf_op jit(solution)/shard_map/ppermute | solution.py:18
  31.1 0.7 copy-start.5
  31.7 21.7 %copy-start.6 = (f32[1,32]{1,0:T(1,128)S(1)}, f32[1,32]{1,0:T(1,128)}, u32[]{:S(2)}) copy-start(f32[1,32]{1,0:T(1,128)} %param.13) | copy-start | bytes 388
  31.9 21.5 %collective-permute-start.4 = (f32[32,2,32,128]{3,2,1,0:T(8,128)S(1)}, f32[32,2,32,128]{3,2,1,0:T(8,128)S(1)}, u32[]{:S(2)}, u32[]{:S(2)}) collective-permute-start(f32[32,2,32,128]{3,2,1,0:T(8,128)S(1)} %broadcast_multiply_fusion), channel_id=1, source_target_pairs={{0,8},{8,16},{16,24},{1,9},{9,17},{17,25},{2,10},{10,18},{18,26},{... | collective-permute-start | bytes 3145736 | tf_op jit(solution)/shard_map/ppermute | solution.py:30
  53.6 23.5 %collective-permute-start.5 = (f32[32,2,32,128]{3,2,1,0:T(8,128)S(1)}, f32[32,2,32,128]{3,2,1,0:T(8,128)S(1)}, u32[]{:S(2)}, u32[]{:S(2)}) collective-permute-start(f32[32,2,32,128]{3,2,1,0:T(8,128)S(1)} %multiply_add_fusion.2), channel_id=1, source_target_pairs={{0,8},{8,16},{16,24},{1,9},{9,17},{17,25},{2,10},{10,18},{18,26},{... | collective-permute-start | bytes 3145736 | tf_op jit(solution)/shard_map/ppermute | solution.py:30
  77.3 24.6 %collective-permute-start.6 = (f32[32,2,32,128]{3,2,1,0:T(8,128)S(1)}, f32[32,2,32,128]{3,2,1,0:T(8,128)S(1)}, u32[]{:S(2)}, u32[]{:S(2)}) collective-permute-start(f32[32,2,32,128]{3,2,1,0:T(8,128)S(1)} %multiply_add_fusion.1), channel_id=1, source_target_pairs={{0,8},{8,16},{16,24},{1,9},{9,17},{17,25},{2,10},{10,18},{18,26},{... | collective-permute-start | bytes 3145736 | tf_op jit(solution)/shard_map/ppermute | solution.py:30
  102.1 1.0 copy-start.2
  103.1 0.7 copy-start.8
  103.3 2.0 %copy-start.9 = (s32[1,8]{1,0:T(1,128)S(1)}, s32[1,8]{1,0:T(1,128)}, u32[]{:S(2)}) copy-start(s32[1,8]{1,0:T(1,128)} %param.17) | copy-start | bytes 100
Sparse Core Ops, SparseCore 0:
  106.6 57.1 reduce-scatter.1
where the time goes:
time: 191 us
  waiting for transfers between devices  118 us (62%)
  starting transfers between devices  28.5 us (15%)
  blocking collectives  20.2 us (11%)
  between operations  14.3 us (7%)
  matrix products  4.16 us (2%)
  local copies, waits for them, and re-layouts  3.81 us (2%)
  other arithmetic  2.35 us (1%)
    reduce_scatter x1, waiting for transfers between devices, body(): sky = lax.psum_scatter(summed, 'space', scatter_dimension=0, tiled=True)  57.4 us
    ppermute x3, waiting for transfers between devices, from_behind(): return lax.ppermute(block, axis, route)  57.2 us
    psum x1, blocking collectives, body(): summed = lax.psum(dense_map, 'species')  20.2 us
    ppermute x2, starting transfers between devices, padded_2(): lax.ppermute(tail, axis, [(i, (i + 1) % count) for i in range(ends)])  13.5 us
    ppermute x3, starting transfers between devices, from_behind(): return lax.ppermute(block, axis, route)  12.5 us
  transfers between devices with their start and end apart: 8, of which 6 were waited for; matrix products, arithmetic and copies ran while one was open for 0% of the time, Pallas kernels for 0%

commit v1 on v0

--- a/solution.py
+++ b/solution.py
@@ -88,7 +88,7 @@
     dense_map = jnp.dot(
         onehot.T, contribution, precision=lax.Precision.HIGHEST, preferred_element_type=jnp.float32
     )
-    summed = lax.psum(dense_map, "species")
+    summed = jnp.sum(lax.all_gather(dense_map, axis_name="species"), 0)
     sky = lax.psum_scatter(summed, "space", scatter_dimension=0, tiled=True)
     return (carried[None], sky)
 

time: 191 us -> 189 us (0.990)
  waiting for transfers between devices: 118 us -> 116 us
    psum x1 -> x0, blocking collectives: 20.2 us -> none  [body(): summed = lax.psum(dense_map, 'species')]
    all_gather x0 -> x1, blocking collectives: none -> 19.2 us  [body(): summed = jnp.sum(lax.all_gather(dense_map, axis_name='species'), 0)]
where the time goes in v1:
time: 189 us; the launch traced here: 188 us
  waiting for transfers between devices  116 us (61%)
  starting transfers between devices  28.5 us (15%)
  blocking collectives  19.2 us (10%)
  between operations  14.3 us (8%)
  local copies, waits for them, and re-layouts  3.81 us (2%)
  matrix products  3.47 us (2%)
  other arithmetic  3.07 us (2%)
    ppermute x3, waiting for transfers between devices, from_behind(): return lax.ppermute(block, axis, route)  57.2 us
    reduce_scatter x1, waiting for transfers between devices, body(): sky = lax.psum_scatter(summed, 'space', scatter_dimension=0, tiled=True)  55.8 us
    all_gather x1, blocking collectives, body(): summed = jnp.sum(lax.all_gather(dense_map, axis_name='species'), 0)  19.2 us
    ppermute x2, starting transfers between devices, padded_2(): lax.ppermute(tail, axis, [(i, (i + 1) % count) for i in range(ends)])  13.5 us
    ppermute x3, starting transfers between devices, from_behind(): return lax.ppermute(block, axis, route)  12.5 us
  transfers between devices with their start and end apart: 8, of which 6 were waited for; matrix products, arithmetic and copies ran while one was open for 0% of the time, Pallas kernels for 0%

profile of v1, /device:TPU:0, one launch (start us, length us, event | category | flops | bytes accessed | tf_op | source)
XLA Modules:
  0.0 188.3 jit_solution(13211925934727204894)
XLA Ops:
  7.2 0.0 copy-start
  7.2 0.0 reduce-scatter.2.cloned.1.call-start
  7.2 0.0 copy-start.1
  7.2 0.0 copy-start.3
  7.2 0.0 copy-start.7
  7.3 1.4 fusion.25
  8.6 1.3 collective-permute-start
  9.9 3.1 %collective-permute-start.1 = (f32[32,1,32,128]{3,2,1,0:T(8,128)S(1)}, f32[32,1,32,128]{3,2,1,0:T(8,128)S(1)}, u32[]{:S(2)}, u32[]{:S(2)}) collective-permute-start(f32[32,1,32,128]{3,2,1,0:T(8,128)S(1)} %get-tuple-element.5), channel_id=1, source_target_pairs={{0,1},{1,2},{2,3},{3,4},{4,5},{5,6},{6,7},{8,9},{9,10},{10,11},{11... | collective-permute-start | bytes 1572872 | tf_op jit(solution)/shard_map/ppermute | solution.py:18
  13.0 0.0 collective-permute-done
  13.0 1.5 collective-permute-done.1
  14.5 0.0 copy-done.1
  14.5 0.0 copy-done.3
  14.5 0.0 copy-done.7
  14.5 0.8 fusion
  15.3 0.1 fusion.24
  15.4 1.3 collective-permute-start.2
  16.7 0.0 copy-start.4
  16.7 10.4 %collective-permute-start.3 = (f32[32,1,32,128]{3,2,1,0:T(8,128)S(1)}, f32[32,1,32,128]{3,2,1,0:T(8,128)S(1)}, u32[]{:S(2)}, u32[]{:S(2)}) collective-permute-start(f32[32,1,32,128]{3,2,1,0:T(8,128)S(1)} %get-tuple-element.3), channel_id=1, source_target_pairs={{0,1},{1,2},{2,3},{3,4},{4,5},{5,6},{6,7},{8,9},{9,10},{10,11},{11... | collective-permute-start | bytes 1572872 | tf_op jit(solution)/shard_map/ppermute | solution.py:18
  27.1 0.0 collective-permute-done.2
  27.1 1.5 collective-permute-done.3
  28.6 0.8 fusion.1
  29.4 0.0 copy-done.4
  29.4 1.7 convolution_bitcast_fusion
  31.1 0.0 copy-start.5
  31.1 0.2 copy.16
  31.3 0.5 copy-done.5
  31.7 0.0 copy-start.6
  31.7 0.1 broadcast_multiply_fusion
  31.9 3.5 %collective-permute-start.4 = (f32[32,2,32,128]{3,2,1,0:T(8,128)S(1)}, f32[32,2,32,128]{3,2,1,0:T(8,128)S(1)}, u32[]{:S(2)}, u32[]{:S(2)}) collective-permute-start(f32[32,2,32,128]{3,2,1,0:T(8,128)S(1)} %broadcast_multiply_fusion), channel_id=1, source_target_pairs={{0,8},{8,16},{16,24},{1,9},{9,17},{17,25},{2,10},{10,18},{18,26},{... | collective-permute-start | bytes 3145736 | tf_op jit(solution)/shard_map/ppermute | solution.py:30
  35.4 18.0 %collective-permute-done.4 = f32[32,2,32,128]{3,2,1,0:T(8,128)S(1)} collective-permute-done((f32[32,2,32,128]{3,2,1,0:T(8,128)S(1)}, f32[32,2,32,128]{3,2,1,0:T(8,128)S(1)}, u32[]{:S(2)}, u32[]{:S(2)}) %collective-permute-start.4) | collective-permute-done | bytes 1048608 | tf_op jit(solution)/shard_map/ppermute | solution.py:30
  53.4 0.0 copy-done.6
  53.4 0.2 multiply_add_fusion.2
  53.6 4.5 %collective-permute-start.5 = (f32[32,2,32,128]{3,2,1,0:T(8,128)S(1)}, f32[32,2,32,128]{3,2,1,0:T(8,128)S(1)}, u32[]{:S(2)}, u32[]{:S(2)}) collective-permute-start(f32[32,2,32,128]{3,2,1,0:T(8,128)S(1)} %multiply_add_fusion.2), channel_id=1, source_target_pairs={{0,8},{8,16},{16,24},{1,9},{9,17},{17,25},{2,10},{10,18},{18,26},{... | collective-permute-start | bytes 3145736 | tf_op jit(solution)/shard_map/ppermute | solution.py:30
  58.1 19.1 %collective-permute-done.5 = f32[32,2,32,128]{3,2,1,0:T(8,128)S(1)} collective-permute-done((f32[32,2,32,128]{3,2,1,0:T(8,128)S(1)}, f32[32,2,32,128]{3,2,1,0:T(8,128)S(1)}, u32[]{:S(2)}, u32[]{:S(2)}) %collective-permute-start.5) | collective-permute-done | bytes 1048608 | tf_op jit(solution)/shard_map/ppermute | solution.py:30
  77.1 0.2 multiply_add_fusion.1
  77.3 4.5 %collective-permute-start.6 = (f32[32,2,32,128]{3,2,1,0:T(8,128)S(1)}, f32[32,2,32,128]{3,2,1,0:T(8,128)S(1)}, u32[]{:S(2)}, u32[]{:S(2)}) collective-permute-start(f32[32,2,32,128]{3,2,1,0:T(8,128)S(1)} %multiply_add_fusion.1), channel_id=1, source_target_pairs={{0,8},{8,16},{16,24},{1,9},{9,17},{17,25},{2,10},{10,18},{18,26},{... | collective-permute-start | bytes 3145736 | tf_op jit(solution)/shard_map/ppermute | solution.py:30
  81.8 20.1 %collective-permute-done.6 = f32[32,2,32,128]{3,2,1,0:T(8,128)S(1)} collective-permute-done((f32[32,2,32,128]{3,2,1,0:T(8,128)S(1)}, f32[32,2,32,128]{3,2,1,0:T(8,128)S(1)}, u32[]{:S(2)}, u32[]{:S(2)}) %collective-permute-start.6) | collective-permute-done | bytes 1048608 | tf_op jit(solution)/shard_map/ppermute | solution.py:30
  101.9 0.2 multiply_add_fusion
  102.1 0.0 copy-start.2
  102.1 0.6 copy.26
  102.7 0.3 copy-done.2
  103.1 0.0 copy-start.8
  103.1 0.2 copy.18
  103.3 0.0 copy-start.9
  103.3 0.5 copy-done.8
  103.7 1.2 fusion.16
  105.0 0.1 reduce_sum.18
  105.1 0.1 reshape.35
  105.2 0.0 copy-done
  105.2 0.1 fusion.18
  105.3 0.0 copy-done.9
  105.3 0.4 fusion.21
  105.7 19.2 %all-gather = f32[1536,128]{1,0:T(8,128)S(1)} all-gather(f32[384,128]{1,0:T(8,128)S(1)} %fusion.21), channel_id=2, replica_groups=mesh['species'=4,'space'=8] {'species'}, dimensions={0}, use_global_device_ids=true | all-gather | bytes 983040 | tf_op jit(solution)/shard_map/all_gather | solution.py:91
  124.9 0.7 reduce_sum.19
  125.7 0.0 reduce-scatter.2.cloned.1.call-update
  125.7 55.8 %reduce-scatter.2.cloned.1.call-done = f32[48,128]{1,0:T(8,128)} async-done(((f32[384,128]{1,0:T(8,128)}), f32[48,128]{1,0:T(8,128)}) %reduce-scatter.2.cloned.1.call-update) | async-done | bytes 24592 | tf_op jit(solution)/shard_map/reduce_scatter | solution.py:92
  (1 shorter events, 0.0 us)
Async XLA Ops:
  7.2 98.0 %copy-start = (bf16[1,8,64,128]{3,2,1,0:T(8,128)(2,1)S(1)}, bf16[1,8,64,128]{3,2,1,0:T(8,128)(2,1)}, u32[]{:S(2)}) copy-start(bf16[1,8,64,128]{3,2,1,0:T(8,128)(2,1)} %param.16) | copy-start | bytes 393220
  7.2 174.3 %reduce-scatter.2.cloned.1.call-start = ((), (), s32[]{:S(2)}) async-start(), calls=%async_computation.1 | async-start | bytes 221184 | tf_op jit(solution)/shard_map/reduce_scatter | solution.py:92
  7.2 7.3 %copy-start.1 = (f32[1,32,2,32,128]{4,3,2,1,0:T(8,128)S(1)}, f32[1,32,2,32,128]{4,3,2,1,0:T(8,128)}, u32[]{:S(2)}) copy-start(f32[1,32,2,32,128]{4,3,2,1,0:T(8,128)} %param.9) | copy-start | bytes 3145732
  7.2 7.3 %copy-start.3 = (f32[2,32,128]{2,1,0:T(8,128)S(1)}, f32[2,32,128]{2,1,0:T(8,128)}, u32[]{:S(2)}) copy-start(f32[2,32,128]{2,1,0:T(8,128)} %param.10) | copy-start | bytes 98308
  7.2 7.2 %copy-start.7 = (f32[1,32]{1,0:T(1,128)S(1)}, f32[1,32]{1,0:T(1,128)}, u32[]{:S(2)}) copy-start(f32[1,32]{1,0:T(1,128)} %param.11) | copy-start | bytes 388
  8.6 4.4 %collective-permute-start = (f32[32,1,32,128]{3,2,1,0:T(8,128)S(1)}, f32[32,1,32,128]{3,2,1,0:T(8,128)S(1)}, u32[]{:S(2)}, u32[]{:S(2)}) collective-permute-start(f32[32,1,32,128]{3,2,1,0:T(8,128)S(1)} %get-tuple-element.4), channel_id=1, source_target_pairs={{1,0},{2,1},{3,2},{4,3},{5,4},{6,5},{7,6},{9,8},{10,9},{11,10},{12... | collective-permute-start | bytes 1572872 | tf_op jit(solution)/shard_map/ppermute | solution.py:20
  9.9 4.6 %collective-permute-start.1 = (f32[32,1,32,128]{3,2,1,0:T(8,128)S(1)}, f32[32,1,32,128]{3,2,1,0:T(8,128)S(1)}, u32[]{:S(2)}, u32[]{:S(2)}) collective-permute-start(f32[32,1,32,128]{3,2,1,0:T(8,128)S(1)} %get-tuple-element.5), channel_id=1, source_target_pairs={{0,1},{1,2},{2,3},{3,4},{4,5},{5,6},{6,7},{8,9},{9,10},{10,11},{11... | collective-permute-start | bytes 1572872 | tf_op jit(solution)/shard_map/ppermute | solution.py:18
  15.4 11.7 %collective-permute-start.2 = (f32[32,1,32,128]{3,2,1,0:T(8,128)S(1)}, f32[32,1,32,128]{3,2,1,0:T(8,128)S(1)}, u32[]{:S(2)}, u32[]{:S(2)}) collective-permute-start(f32[32,1,32,128]{3,2,1,0:T(8,128)S(1)} %get-tuple-element.2), channel_id=1, source_target_pairs={{1,0},{2,1},{3,2},{4,3},{5,4},{6,5},{7,6},{9,8},{10,9},{11,10},{12... | collective-permute-start | bytes 1572872 | tf_op jit(solution)/shard_map/ppermute | solution.py:20
  16.7 12.7 %copy-start.4 = (f32[1,32,32]{2,1,0:T(8,128)S(1)}, f32[1,32,32]{2,1,0:T(8,128)}, u32[]{:S(2)}) copy-start(f32[1,32,32]{2,1,0:T(8,128)} %param.12) | copy-start | bytes 12292
  16.7 11.9 %collective-permute-start.3 = (f32[32,1,32,128]{3,2,1,0:T(8,128)S(1)}, f32[32,1,32,128]{3,2,1,0:T(8,128)S(1)}, u32[]{:S(2)}, u32[]{:S(2)}) collective-permute-start(f32[32,1,32,128]{3,2,1,0:T(8,128)S(1)} %get-tuple-element.3), channel_id=1, source_target_pairs={{0,1},{1,2},{2,3},{3,4},{4,5},{5,6},{6,7},{8,9},{9,10},{10,11},{11... | collective-permute-start | bytes 1572872 | tf_op jit(solution)/shard_map/ppermute | solution.py:18
  31.1 0.7 copy-start.5
  31.7 21.7 %copy-start.6 = (f32[1,32]{1,0:T(1,128)S(1)}, f32[1,32]{1,0:T(1,128)}, u32[]{:S(2)}) copy-start(f32[1,32]{1,0:T(1,128)} %param.13) | copy-start | bytes 388
  31.9 21.5 %collective-permute-start.4 = (f32[32,2,32,128]{3,2,1,0:T(8,128)S(1)}, f32[32,2,32,128]{3,2,1,0:T(8,128)S(1)}, u32[]{:S(2)}, u32[]{:S(2)}) collective-permute-start(f32[32,2,32,128]{3,2,1,0:T(8,128)S(1)} %broadcast_multiply_fusion), channel_id=1, source_target_pairs={{0,8},{8,16},{16,24},{1,9},{9,17},{17,25},{2,10},{10,18},{18,26},{... | collective-permute-start | bytes 3145736 | tf_op jit(solution)/shard_map/ppermute | solution.py:30
  53.6 23.5 %collective-permute-start.5 = (f32[32,2,32,128]{3,2,1,0:T(8,128)S(1)}, f32[32,2,32,128]{3,2,1,0:T(8,128)S(1)}, u32[]{:S(2)}, u32[]{:S(2)}) collective-permute-start(f32[32,2,32,128]{3,2,1,0:T(8,128)S(1)} %multiply_add_fusion.2), channel_id=1, source_target_pairs={{0,8},{8,16},{16,24},{1,9},{9,17},{17,25},{2,10},{10,18},{18,26},{... | collective-permute-start | bytes 3145736 | tf_op jit(solution)/shard_map/ppermute | solution.py:30
  77.3 24.6 %collective-permute-start.6 = (f32[32,2,32,128]{3,2,1,0:T(8,128)S(1)}, f32[32,2,32,128]{3,2,1,0:T(8,128)S(1)}, u32[]{:S(2)}, u32[]{:S(2)}) collective-permute-start(f32[32,2,32,128]{3,2,1,0:T(8,128)S(1)} %multiply_add_fusion.1), channel_id=1, source_target_pairs={{0,8},{8,16},{16,24},{1,9},{9,17},{17,25},{2,10},{10,18},{18,26},{... | collective-permute-start | bytes 3145736 | tf_op jit(solution)/shard_map/ppermute | solution.py:30
  102.1 1.0 copy-start.2
  103.1 0.7 copy-start.8
  103.3 2.0 %copy-start.9 = (s32[1,8]{1,0:T(1,128)S(1)}, s32[1,8]{1,0:T(1,128)}, u32[]{:S(2)}) copy-start(s32[1,8]{1,0:T(1,128)} %param.17) | copy-start | bytes 100
Sparse Core Ops, SparseCore 0:
  125.8 55.6 reduce-scatter.1
